TPU v7x, 256 devices: a whole 4x4x8 slice. The times are simulated.
256 devices in a mesh: wave: 8 (over z_hi, x), region: 32 (over z_lo, y, core).
Axes of the slice: x: 4, y: 4, z: 8 (z_hi: 2, z_lo: 4; z = z_hi * 4 + z_lo), core: 2. Of those that a mesh axis runs over, the one named last changes fastest.
Arguments:
- object_field: float32 [2, 16384, 1024], P(None, 'region'), may hold values from -5 to 5
- probes: float32 [8, 2, 256, 256], P('wave'), may hold values from -5 to 5
- patterns: bfloat16 [8, 512, 256, 256], P('wave', 'region'), may hold values from 0 to 2
- offsets: int32 [512, 2], P('region'), may hold values from 0 to 768, as said below
- counts: int32 [32], P('region'), may hold values from 1 to 16, as said below
Outputs:
- object_grad: float32 [2, 16384, 1024], P(None, 'region', 'wave')
- probe_grad: float32 [8, 2, 256, 256], P('wave')
Inputs may be any that keep to these rules, and one draw needn't show every extreme that they name: Offsets are whole cells: row offsets below 512, column offsets at most 768. `counts`: some tile uses all slots and some tile uses one.
All inputs are finite; a program needn't handle non-finite values.
Results may differ from a plain program's by a relative error of at most 0.0052.
Values sent between devices are 32-bit elements; how exact they have to be, the bound alone decides.
No kernel may reach another device: no remote copies, remote signals or barrier semaphores. Data moves between devices by JAX's collectives and lax.ppermute only.
A program may use at most 128 MiB of HBM per device.

v0:
```python
import math
import jax
import jax.numpy as jnp
from jax import lax
from jax.sharding import PartitionSpec as P


def from_behind(block, axis, distance):
    devices = range(lax.axis_size(axis))
    route = [(i - distance, i) for i in devices if i - distance in devices]
    return lax.ppermute(block, axis, route)


def make_tables(patch_side):
    index = jnp.arange(patch_side, dtype=jnp.int32)
    phase_int = index[:, None] * index[None, :] % patch_side
    phase = phase_int.astype(jnp.float32) * (2.0 * math.pi / patch_side)
    scale = 1.0 / math.sqrt(patch_side)
    return (
        (jnp.cos(phase) * scale).astype(jnp.bfloat16),
        (jnp.sin(phase) * scale).astype(jnp.bfloat16),
    )


def apply_left(table, field_part):
    return jnp.einsum("kn,bnm->bkm", table, field_part, preferred_element_type=jnp.float32)


def apply_right(field_part, table):
    return jnp.einsum("bkn,nm->bkm", field_part, table, preferred_element_type=jnp.float32)


def on_device(object_field, probes, patterns, offsets, counts):
    tile_rows = object_field.shape[1]
    width_cols = object_field.shape[2]
    patch_side = probes.shape[-1]
    slot_total = offsets.shape[0]
    top_rows = object_field[:, :patch_side, :]
    rim_rows = from_behind(top_rows, "region", -1)
    extended = jnp.concatenate([object_field, rim_rows], axis=1)
    zero_at = jnp.zeros((), jnp.int32)

    def extract(row_at, col_at):
        return lax.dynamic_slice(extended, (zero_at, row_at, col_at), (2, patch_side, patch_side))

    patches = jax.vmap(extract)(offsets[:, 0], offsets[:, 1])
    cos_table, sin_table = make_tables(patch_side)
    probe_re = probes[0, 0]
    probe_im = probes[0, 1]
    wave_re = (probe_re * patches[:, 0] - probe_im * patches[:, 1]).astype(jnp.bfloat16)
    wave_im = (probe_re * patches[:, 1] + probe_im * patches[:, 0]).astype(jnp.bfloat16)
    half_re = (apply_left(cos_table, wave_re) + apply_left(sin_table, wave_im)).astype(jnp.bfloat16)
    half_im = (apply_left(cos_table, wave_im) - apply_left(sin_table, wave_re)).astype(jnp.bfloat16)
    far_re = apply_right(half_re, cos_table) + apply_right(half_im, sin_table)
    far_im = apply_right(half_im, cos_table) - apply_right(half_re, sin_table)
    excess = far_re * far_re + far_im * far_im - patterns[0].astype(jnp.float32)
    back_re = (excess * far_re).astype(jnp.bfloat16)
    back_im = (excess * far_im).astype(jnp.bfloat16)
    inner_re = (apply_left(cos_table, back_re) - apply_left(sin_table, back_im)).astype(
        jnp.bfloat16
    )
    inner_im = (apply_left(cos_table, back_im) + apply_left(sin_table, back_re)).astype(
        jnp.bfloat16
    )
    chi_re = apply_right(inner_re, cos_table) - apply_right(inner_im, sin_table)
    chi_im = apply_right(inner_im, cos_table) + apply_right(inner_re, sin_table)
    in_use = (jnp.arange(slot_total, dtype=jnp.int32) < counts[0]).astype(jnp.float32)[
        :, None, None
    ]
    obj_terms = jnp.stack(
        [
            (probe_re * chi_re + probe_im * chi_im) * in_use,
            (probe_re * chi_im - probe_im * chi_re) * in_use,
        ],
        axis=1,
    )
    prb_re = jnp.sum((patches[:, 0] * chi_re + patches[:, 1] * chi_im) * in_use, axis=0)
    prb_im = jnp.sum((patches[:, 0] * chi_im - patches[:, 1] * chi_re) * in_use, axis=0)
    probe_total = lax.psum(jnp.stack([prb_re, prb_im]), "region")

    def accumulate(slot, grad_ext):
        row_at = offsets[slot, 0]
        col_at = offsets[slot, 1]
        current = lax.dynamic_slice(
            grad_ext, (zero_at, row_at, col_at), (2, patch_side, patch_side)
        )
        return lax.dynamic_update_slice(
            grad_ext, current + obj_terms[slot], (zero_at, row_at, col_at)
        )

    grad_ext = lax.fori_loop(
        0, slot_total, accumulate, jnp.zeros((2, tile_rows + patch_side, width_cols), jnp.float32)
    )
    arrived = from_behind(grad_ext[:, tile_rows:, :], "region", 1)
    tile_grad = grad_ext[:, :tile_rows, :] + jnp.pad(
        arrived, ((0, 0), (0, tile_rows - patch_side), (0, 0))
    )
    object_out = lax.psum_scatter(tile_grad, "wave", scatter_dimension=2, tiled=True)
    return (object_out, probe_total[None])


def solution(mesh):
    in_specs = (
        P(None, "region", None),
        P("wave", None, None, None),
        P("wave", "region", None, None),
        P("region", None),
        P("region"),
    )
    out_specs = (P(None, "region", "wave"), P("wave", None, None, None))
    return jax.shard_map(
        on_device, mesh=mesh, in_specs=in_specs, out_specs=out_specs, check_vma=False
    )
```

profile of v0, /device:TPU:1, one launch (start us, length us, event | category | flops | bytes accessed | tf_op | source)
XLA Modules:
  0.0 687.2 jit_solution(8466488751038629927)
XLA Ops:
  8.1 1.8 slice.34
  9.8 5.1 collective-permute-start
  15.8 22.5 %collective-permute-done = f32[2,256,1024]{2,1,0:T(8,128)} collective-permute-done((f32[2,256,1024]{2,1,0:T(8,128)S(1)}, f32[2,256,1024]{2,1,0:T(8,128)}, u32[]{:S(2)}, u32[]{:S(2)}) %collective-permute-start) | collective-permute-done | bytes 2097184 | tf_op jit(solution)/shard_map/ppermute | solution.py:11
  38.2 6.7 pad_maximum_fusion.1
  44.9 63.9 %while.15 = (s32[]{:T(128)}, f32[2,768,1024]{2,1,0:T(8,128)}, s32[16,3]{0,1:T(4,128)S(1)}, f32[16,2,256,256]{3,2,0,1:T(8,128)}, s32[]{:T(128)}) while((s32[]{:T(128)}, f32[2,768,1024]{2,1,0:T(8,128)}, s32[16,3]{0,1:T(4,128)S(1)}, f32[16,2,256,256]{3,2,0,1:T(8,128)}, s32[]{:T(128)}) %tuple.58), condition=%wide.while_cond, body=%wide.while_body.sunk | while | flops 2 | bytes 1050217 | solution.py:44
  45.5 3.3 bitcast_dynamic-update-slice_fusion.2
  49.5 3.3 bitcast_dynamic-update-slice_fusion.2
  53.5 3.4 bitcast_dynamic-update-slice_fusion.2
  57.5 3.4 bitcast_dynamic-update-slice_fusion.2
  61.5 3.4 bitcast_dynamic-update-slice_fusion.2
  65.5 3.4 bitcast_dynamic-update-slice_fusion.2
  69.5 3.4 bitcast_dynamic-update-slice_fusion.2
  73.5 3.4 bitcast_dynamic-update-slice_fusion.2
  77.5 3.3 bitcast_dynamic-update-slice_fusion.2
  81.5 3.4 bitcast_dynamic-update-slice_fusion.2
  85.5 3.4 bitcast_dynamic-update-slice_fusion.2
  89.5 3.3 bitcast_dynamic-update-slice_fusion.2
  93.4 3.3 bitcast_dynamic-update-slice_fusion.2
  97.4 3.3 bitcast_dynamic-update-slice_fusion.2
  101.4 3.4 bitcast_dynamic-update-slice_fusion.2
  105.4 3.4 bitcast_dynamic-update-slice_fusion.2
  108.8 4.7 fusion.3
  113.5 1.7 fusion.45
  115.1 1.7 fusion.48
  116.8 1.7 subtract_convert_fusion.1
  118.5 1.7 add_convert_fusion.1
  120.2 1.7 fusion.20
  121.9 1.7 fusion.16
  123.6 1.9 convolution_add_fusion.1
  125.5 2.9 multiply_convert_fusion
  128.4 1.7 fusion.42
  130.1 1.7 fusion.39
  131.7 1.7 subtract_convert_fusion
  133.5 1.7 add_convert_fusion
  135.1 1.7 fusion.10
  136.8 1.7 fusion.14
  138.5 1.7 convolution_add_fusion
  140.8 6.6 fusion.6
  147.4 4.1 pad_maximum_fusion
  151.5 3.5 broadcast_in_dim.4
  155.0 202.1 %while.14 = (s32[]{:T(128)}, f32[2,768,1024]{2,1,0:T(8,128)}, s32[16,2]{0,1:T(2,128)S(1)}, f32[16,2,256,256]{3,2,0,1:T(8,128)}, s32[]{:T(128)}, /*index=5*/s32[]{:T(128)}, s32[]{:T(128)}, s32[]{:T(128)}) while((s32[]{:T(128)}, f32[2,768,1024]{2,1,0:T(8,128)}, s32[16,2]{0,1:T(2,128)S(1)}, f32[16,2,256,256]{3,2,0,1:T(8,128)}, s32[]{:T(128)}, ...), condition=%wide.region_1.2_spmd, body=%wide.region_0.1_spmd.sunk | while | flops 131080 | bytes 2621629 | solution.py:91
  161.1 6.8 dynamic_update_slice.8
  173.8 6.8 dynamic_update_slice.8
  185.1 1.5 bitcast_add_fusion.2
  186.6 6.8 dynamic_update_slice.8
  199.4 6.2 dynamic_update_slice.8
  211.6 6.2 dynamic_update_slice.8
  223.8 6.8 dynamic_update_slice.8
  236.6 6.7 dynamic_update_slice.8
  249.3 6.8 dynamic_update_slice.8
  262.1 6.8 dynamic_update_slice.8
  274.9 6.5 dynamic_update_slice.8
  287.4 6.1 dynamic_update_slice.8
  299.5 6.8 dynamic_update_slice.8
  312.3 6.5 dynamic_update_slice.8
  324.8 6.8 dynamic_update_slice.8
  337.6 6.7 dynamic_update_slice.8
  350.3 6.8 dynamic_update_slice.8
  357.1 3.2 slice.41
  360.4 1.9 collective-permute-start.1
  363.2 22.5 %collective-permute-done.1 = f32[2,256,1024]{2,1,0:T(8,128)S(1)} collective-permute-done((f32[2,256,1024]{2,1,0:T(8,128)}, f32[2,256,1024]{2,1,0:T(8,128)S(1)}, u32[]{:S(2)}, u32[]{:S(2)}) %collective-permute-start.1) | collective-permute-done | bytes 2097184 | tf_op jit(solution)/shard_map/ppermute | solution.py:11
  385.7 5.0 pad_add_fusion
  390.8 287.1 %all-reduce.3.cloned.1.call-done = f32[1,2,256,256]{3,2,1,0:T(8,128)} async-done(((f32[1,2,256,256]{3,2,1,0:T(8,128)}), f32[1,2,256,256]{3,2,1,0:T(8,128)}) %all-reduce.3.cloned.1.call-update) | async-done | bytes 524304 | tf_op jit(solution)/shard_map/psum | solution.py:79
  677.9 1.9 copy.64
  (94 shorter events, 44.3 us)
Async XLA Ops:
  8.0 7.6 %copy-start.6 = (s32[16,2]{0,1:T(2,128)S(1)}, s32[16,2]{0,1:T(2,128)}, u32[]{:S(2)}) copy-start(s32[16,2]{0,1:T(2,128)} %param.10) | copy-start | bytes 388
  8.0 7.7 %copy-start.3 = (f32[1,2,256,256]{3,2,1,0:T(8,128)S(1)}, f32[1,2,256,256]{3,2,1,0:T(8,128)}, u32[]{:S(2)}) copy-start(f32[1,2,256,256]{3,2,1,0:T(8,128)} %param.8) | copy-start | bytes 1572868
  8.0 669.9 %all-reduce.3.cloned.1.call-start = ((), (), s32[]{:S(2)}) async-start(), calls=%async_computation.2 | async-start | bytes 1048576 | tf_op jit(solution)/shard_map/psum | solution.py:79
  9.8 28.4 %collective-permute-start = (f32[2,256,1024]{2,1,0:T(8,128)S(1)}, f32[2,256,1024]{2,1,0:T(8,128)}, u32[]{:S(2)}, u32[]{:S(2)}) collective-permute-start(f32[2,256,1024]{2,1,0:T(8,128)S(1)} %slice.34), channel_id=1, source_target_pairs={{1,0},{2,1},{3,2},{4,3},{5,4},{6,5},{7,6},{8,7},{9,8},{10,9},{11,1... | collective-permute-start | bytes 6291464 | tf_op jit(solution)/shard_map/ppermute | solution.py:11
  15.7 93.0 %copy-start.1 = (f32[256,256]{1,0:T(8,128)}, f32[256,256]{1,0:T(8,128)S(1)}, u32[]{:S(2)}) copy-start(f32[256,256]{1,0:T(8,128)S(1)} %get-tuple-element.124) | copy-start | bytes 786436
  15.7 93.0 %copy-start.2 = (f32[256,256]{1,0:T(8,128)}, f32[256,256]{1,0:T(8,128)S(1)}, u32[]{:S(2)}) copy-start(f32[256,256]{1,0:T(8,128)S(1)} %get-tuple-element.125) | copy-start | bytes 786436
  123.6 1.9 copy-start
  136.8 3.4 slice-start
  138.5 2.3 slice-start.1
  357.1 5.2 copy-start.4
  357.1 5.2 copy-start.5
  360.4 25.4 %collective-permute-start.1 = (f32[2,256,1024]{2,1,0:T(8,128)}, f32[2,256,1024]{2,1,0:T(8,128)S(1)}, u32[]{:S(2)}, u32[]{:S(2)}) collective-permute-start(f32[2,256,1024]{2,1,0:T(8,128)} %slice.41), channel_id=1, source_target_pairs={{0,1},{1,2},{2,3},{3,4},{4,5},{5,6},{6,7},{7,8},{8,9},{9,10},{10,1... | collective-permute-start | bytes 6291464 | tf_op jit(solution)/shard_map/ppermute | solution.py:11
  363.2 314.7 %reduce-scatter.2.cloned.1.call-start = ((), (), s32[]{:S(2)}) async-start(), calls=%async_computation.1 | async-start | bytes 4718592 | tf_op jit(solution)/shard_map/reduce_scatter | solution.py:98
Sparse Core Ops, SparseCore 0:
  363.3 314.5 all-reduce.2
Sparse Core Ops, SparseCore 1:
  390.8 125.0 reduce-scatter.1
where the time goes:
time: 692 us; the launch traced here: 687 us
  waiting for transfers between devices  332 us (48%)
  local copies, waits for them, and re-layouts  190 us (27%)
  loops' own time  62.2 us (9%)
  other arithmetic  45.8 us (7%)
  matrix products  33.2 us (5%)
  between operations  16.4 us (2%)
  starting transfers between devices  7.1 us (1%)
    psum x1, waiting for transfers between devices, on_device(): probe_total = lax.psum(jnp.stack([prb_re, prb_im]), 'region')  287 us
    dynamic_update_slice x16, local copies, waits for them, and re-layouts, accumulate(): lax.dynamic_update_slice(grad_ext, current + obj_terms[slot], (zero_at, r...  106 us
    gather x48, local copies, waits for them, and re-layouts  63.9 us
    another operation x1, loops' own time, on_device(): lax.fori_loop(0, slot_total, accumulate, jnp.zeros((2, tile_rows + patch_...  62.2 us
    ppermute x2, waiting for transfers between devices, from_behind(): return lax.ppermute(block, axis, route)  45 us
    add x16, other arithmetic, accumulate(): current + obj_terms[slot]  24.5 us
    dot_general x8, matrix products, apply_right(): jnp.einsum('bkn,nm->bkm', field_part, table, preferred_element_type=jnp.f...  19.7 us
  transfers between devices with their start and end apart: 4, of which 3 were waited for; matrix products, arithmetic and copies ran while one was open for 1% of the time, Pallas kernels for 0%

commit v1 on v0

--- a/solution.py
+++ b/solution.py
@@ -76,7 +76,9 @@
     )
     prb_re = jnp.sum((patches[:, 0] * chi_re + patches[:, 1] * chi_im) * in_use, axis=0)
     prb_im = jnp.sum((patches[:, 0] * chi_im - patches[:, 1] * chi_re) * in_use, axis=0)
-    probe_total = lax.psum(jnp.stack([prb_re, prb_im]), "region")
+    x = jnp.stack([prb_re, prb_im])
+    parts = lax.all_gather(x, "region")
+    probe_total = jnp.sum(parts, axis=0)
 
     def accumulate(slot, grad_ext):
         row_at = offsets[slot, 0]

time: 692 us -> 541 us (0.78)
  waiting for transfers between devices: 332 us -> 165 us
  other arithmetic: 45.8 us -> 57.5 us
    psum x1 -> x0, waiting for transfers between devices: 287 us -> none  [on_device(): probe_total = lax.psum(jnp.stack([prb_re, prb_im]), 'region')]
    reduce_scatter x1, waiting for transfers between devices: 0.01 us -> 120 us  [on_device(): lax.psum_scatter(tile_grad, 'wave', scatter_dimension=2, tiled=True)]
    reduce_sum x0 -> x1, other arithmetic: none -> 7.69 us  [on_device(): probe_total = jnp.sum(parts, axis=0)]
  transfers between devices with their start and end apart: 4 -> 4, of which waited for: 3 -> 3; matrix products, arithmetic and copies ran while one was open for 1% -> 31% of each run, Pallas kernels for 0% -> 0%
where the time goes in v1:
time: 541 us; the launch traced here: 535 us
  local copies, waits for them, and re-layouts  191 us (35%)
  waiting for transfers between devices  165 us (30%)
  loops' own time  63.8 us (12%)
  other arithmetic  57.5 us (11%)
  matrix products  34 us (6%)
  between operations  16.4 us (3%)
  starting transfers between devices  7.11 us (1%)
    reduce_scatter x1, waiting for transfers between devices, on_device(): lax.psum_scatter(tile_grad, 'wave', scatter_dimension=2, tiled=True)  120 us
    dynamic_update_slice x16, local copies, waits for them, and re-layouts, accumulate(): lax.dynamic_update_slice(grad_ext, current + obj_terms[slot], (zero_at, r...  106 us
    gather x48, local copies, waits for them, and re-layouts  66.6 us
    another operation x1, loops' own time, on_device(): lax.fori_loop(0, slot_total, accumulate, jnp.zeros((2, tile_rows + patch_...  63.8 us
    ppermute x2, waiting for transfers between devices, from_behind(): return lax.ppermute(block, axis, route)  45.5 us
    add x16, other arithmetic, accumulate(): current + obj_terms[slot]  25 us
    dot_general x8, matrix products, apply_right(): jnp.einsum('bkn,nm->bkm', field_part, table, preferred_element_type=jnp.f...  20.5 us
    dot_general x8, matrix products, apply_left(): jnp.einsum('kn,bnm->bkm', table, field_part, preferred_element_type=jnp.f...  13.5 us
  transfers between devices with their start and end apart: 4, of which 3 were waited for; matrix products, arithmetic and copies ran while one was open for 31% of the time, Pallas kernels for 0%

profile of v1, /device:TPU:1, one launch (start us, length us, event | category | flops | bytes accessed | tf_op | source)
XLA Modules:
  0.0 534.8 jit_solution(3981517262395758004)
XLA Ops:
  8.1 1.8 slice.34
  9.8 5.1 collective-permute-start
  15.7 22.5 %collective-permute-done = f32[2,256,1024]{2,1,0:T(8,128)} collective-permute-done((f32[2,256,1024]{2,1,0:T(8,128)S(1)}, f32[2,256,1024]{2,1,0:T(8,128)}, u32[]{:S(2)}, u32[]{:S(2)}) %collective-permute-start) | collective-permute-done | bytes 2097184 | tf_op jit(solution)/shard_map/ppermute | solution.py:11
  38.2 6.6 %pad_maximum_fusion.1 = f32[2,768,1024]{2,1,0:T(8,128)} fusion(f32[2,256,1024]{2,1,0:T(8,128)} %collective-permute-done, f32[2,512,1024]{2,1,0:T(8,128)} %param.7), kind=kLoop, calls=%fused_computation.6 | loop fusion | flops 1572864 | bytes 12582912 | tf_op jit(solution)/shard_map/concatenate | solution.py:40
  44.9 66.6 %while.15 = (s32[]{:T(128)}, f32[2,768,1024]{2,1,0:T(8,128)}, s32[16,3]{0,1:T(4,128)S(1)}, f32[16,2,256,256]{3,2,0,1:T(8,128)}, s32[]{:T(128)}) while((s32[]{:T(128)}, f32[2,768,1024]{2,1,0:T(8,128)}, s32[16,3]{0,1:T(4,128)S(1)}, f32[16,2,256,256]{3,2,0,1:T(8,128)}, s32[]{:T(128)}) %tuple.59), condition=%wide.while_cond, body=%wide.while_body.sunk | while | flops 2 | bytes 1050217 | solution.py:44
  45.6 3.5 bitcast_dynamic-update-slice_fusion.2
  49.7 3.5 bitcast_dynamic-update-slice_fusion.2
  53.9 3.5 bitcast_dynamic-update-slice_fusion.2
  58.1 3.5 bitcast_dynamic-update-slice_fusion.2
  62.2 3.5 bitcast_dynamic-update-slice_fusion.2
  66.4 3.5 bitcast_dynamic-update-slice_fusion.2
  70.6 3.5 bitcast_dynamic-update-slice_fusion.2
  74.7 3.5 bitcast_dynamic-update-slice_fusion.2
  78.9 3.5 bitcast_dynamic-update-slice_fusion.2
  83.0 3.5 bitcast_dynamic-update-slice_fusion.2
  87.2 3.5 bitcast_dynamic-update-slice_fusion.2
  91.3 3.5 bitcast_dynamic-update-slice_fusion.2
  95.5 3.5 bitcast_dynamic-update-slice_fusion.2
  99.6 3.5 bitcast_dynamic-update-slice_fusion.2
  103.8 3.5 bitcast_dynamic-update-slice_fusion.2
  108.0 3.5 bitcast_dynamic-update-slice_fusion.2
  111.5 4.7 fusion.3
  116.2 1.7 fusion.45
  117.8 1.7 fusion.48
  119.5 1.7 subtract_convert_fusion.1
  121.2 1.7 add_convert_fusion.1
  122.9 1.7 fusion.20
  124.6 1.7 fusion.16
  126.3 1.9 convolution_add_fusion.1
  128.2 2.9 multiply_convert_fusion
  131.1 1.7 fusion.42
  132.8 1.7 fusion.39
  134.4 1.7 subtract_convert_fusion
  136.2 1.7 add_convert_fusion
  137.8 1.7 fusion.10
  139.5 1.7 fusion.14
  141.2 1.7 convolution_add_fusion
  143.5 7.4 %fusion.6 = (f32[256,256]{1,0:T(8,128)S(1)}, f32[256,256]{1,0:T(8,128)S(1)}, f32[16,1,256,256]{3,2,0,1:T(8,128)}, f32[16,1,256,256]{3,2,0,1:T(8,128)}) fusion(f32[16,256,256]{2,1,0:T(8,128)S(1)} %convolution_add_fusion, f32[16,2,256,256]{3,2,0,1:T(8,128)S(1)} %bitcast.138, f32[16]{0:T(128)S(1)} %compare_convert_fusion, ...), kind=kOutput, calls=%fused_computation.18 | convolution fusion | flops 557711360 | bytes 28311616 | tf_op jit(solution)/shard_map/bkn,nm->bkm/dot_general | solution.py:30
  151.8 7.6 %pad_maximum_fusion = f32[16,2,256,256]{3,2,0,1:T(8,128)} fusion(f32[16,1,256,256]{3,2,0,1:T(8,128)} %get-tuple-element.126, f32[16,1,256,256]{3,2,0,1:T(8,128)} %get-tuple-element.127), kind=kLoop, calls=%fused_computation.5 | loop fusion | flops 2097152 | bytes 16777216 | tf_op jit(solution)/shard_map/stack | solution.py:70
  159.4 3.5 broadcast_in_dim.4
  162.9 205.5 %while.14 = (s32[]{:T(128)}, f32[2,768,1024]{2,1,0:T(8,128)}, s32[16,2]{0,1:T(2,128)S(1)}, f32[16,2,256,256]{3,2,0,1:T(8,128)}, s32[]{:T(128)}, /*index=5*/s32[]{:T(128)}, s32[]{:T(128)}, s32[]{:T(128)}) while((s32[]{:T(128)}, f32[2,768,1024]{2,1,0:T(8,128)}, s32[16,2]{0,1:T(2,128)S(1)}, f32[16,2,256,256]{3,2,0,1:T(8,128)}, s32[]{:T(128)}, ...), condition=%wide.region_1.2_spmd, body=%wide.region_0.1_spmd.sunk | while | flops 131080 | bytes 2621629 | solution.py:93
  167.5 1.8 bitcast_add_fusion.2
  169.3 6.8 %dynamic_update_slice.8 = f32[2,768,1024]{2,1,0:T(8,128)} dynamic-update-slice(f32[2,768,1024]{2,1,0:T(8,128)} %get-tuple-element.214, f32[2,256,256]{2,1,0:T(8,128)S(1)} %bitcast_add_fusion.2, s32[]{:T(128)} %constant.56.clone.1..sunk, s32[]{:T(128)S(6)} %select_n.104, s32[]{:T(128)S(6)} %select_n.105) | dynamic-update-slice | bytes 1048580 | tf_op jit(solution)/shard_map/while/body/eval_jaxpr/dynamic_update_slice | solution.py:89
  182.2 6.8 %dynamic_update_slice.8 = f32[2,768,1024]{2,1,0:T(8,128)} dynamic-update-slice(f32[2,768,1024]{2,1,0:T(8,128)} %get-tuple-element.214, f32[2,256,256]{2,1,0:T(8,128)S(1)} %bitcast_add_fusion.2, s32[]{:T(128)} %constant.56.clone.1..sunk, s32[]{:T(128)S(6)} %select_n.104, s32[]{:T(128)S(6)} %select_n.105) | dynamic-update-slice | bytes 1048580 | tf_op jit(solution)/shard_map/while/body/eval_jaxpr/dynamic_update_slice | solution.py:89
  195.3 6.8 %dynamic_update_slice.8 = f32[2,768,1024]{2,1,0:T(8,128)} dynamic-update-slice(f32[2,768,1024]{2,1,0:T(8,128)} %get-tuple-element.214, f32[2,256,256]{2,1,0:T(8,128)S(1)} %bitcast_add_fusion.2, s32[]{:T(128)} %constant.56.clone.1..sunk, s32[]{:T(128)S(6)} %select_n.104, s32[]{:T(128)S(6)} %select_n.105) | dynamic-update-slice | bytes 1048580 | tf_op jit(solution)/shard_map/while/body/eval_jaxpr/dynamic_update_slice | solution.py:89
  208.3 6.2 %dynamic_update_slice.8 = f32[2,768,1024]{2,1,0:T(8,128)} dynamic-update-slice(f32[2,768,1024]{2,1,0:T(8,128)} %get-tuple-element.214, f32[2,256,256]{2,1,0:T(8,128)S(1)} %bitcast_add_fusion.2, s32[]{:T(128)} %constant.56.clone.1..sunk, s32[]{:T(128)S(6)} %select_n.104, s32[]{:T(128)S(6)} %select_n.105) | dynamic-update-slice | bytes 1048580 | tf_op jit(solution)/shard_map/while/body/eval_jaxpr/dynamic_update_slice | solution.py:89
  220.7 6.2 %dynamic_update_slice.8 = f32[2,768,1024]{2,1,0:T(8,128)} dynamic-update-slice(f32[2,768,1024]{2,1,0:T(8,128)} %get-tuple-element.214, f32[2,256,256]{2,1,0:T(8,128)S(1)} %bitcast_add_fusion.2, s32[]{:T(128)} %constant.56.clone.1..sunk, s32[]{:T(128)S(6)} %select_n.104, s32[]{:T(128)S(6)} %select_n.105) | dynamic-update-slice | bytes 1048580 | tf_op jit(solution)/shard_map/while/body/eval_jaxpr/dynamic_update_slice | solution.py:89
  233.2 6.8 %dynamic_update_slice.8 = f32[2,768,1024]{2,1,0:T(8,128)} dynamic-update-slice(f32[2,768,1024]{2,1,0:T(8,128)} %get-tuple-element.214, f32[2,256,256]{2,1,0:T(8,128)S(1)} %bitcast_add_fusion.2, s32[]{:T(128)} %constant.56.clone.1..sunk, s32[]{:T(128)S(6)} %select_n.104, s32[]{:T(128)S(6)} %select_n.105) | dynamic-update-slice | bytes 1048580 | tf_op jit(solution)/shard_map/while/body/eval_jaxpr/dynamic_update_slice | solution.py:89
  246.2 6.7 %dynamic_update_slice.8 = f32[2,768,1024]{2,1,0:T(8,128)} dynamic-update-slice(f32[2,768,1024]{2,1,0:T(8,128)} %get-tuple-element.214, f32[2,256,256]{2,1,0:T(8,128)S(1)} %bitcast_add_fusion.2, s32[]{:T(128)} %constant.56.clone.1..sunk, s32[]{:T(128)S(6)} %select_n.104, s32[]{:T(128)S(6)} %select_n.105) | dynamic-update-slice | bytes 1048580 | tf_op jit(solution)/shard_map/while/body/eval_jaxpr/dynamic_update_slice | solution.py:89
  259.1 6.8 %dynamic_update_slice.8 = f32[2,768,1024]{2,1,0:T(8,128)} dynamic-update-slice(f32[2,768,1024]{2,1,0:T(8,128)} %get-tuple-element.214, f32[2,256,256]{2,1,0:T(8,128)S(1)} %bitcast_add_fusion.2, s32[]{:T(128)} %constant.56.clone.1..sunk, s32[]{:T(128)S(6)} %select_n.104, s32[]{:T(128)S(6)} %select_n.105) | dynamic-update-slice | bytes 1048580 | tf_op jit(solution)/shard_map/while/body/eval_jaxpr/dynamic_update_slice | solution.py:89
  272.0 6.8 %dynamic_update_slice.8 = f32[2,768,1024]{2,1,0:T(8,128)} dynamic-update-slice(f32[2,768,1024]{2,1,0:T(8,128)} %get-tuple-element.214, f32[2,256,256]{2,1,0:T(8,128)S(1)} %bitcast_add_fusion.2, s32[]{:T(128)} %constant.56.clone.1..sunk, s32[]{:T(128)S(6)} %select_n.104, s32[]{:T(128)S(6)} %select_n.105) | dynamic-update-slice | bytes 1048580 | tf_op jit(solution)/shard_map/while/body/eval_jaxpr/dynamic_update_slice | solution.py:89
  285.0 6.5 %dynamic_update_slice.8 = f32[2,768,1024]{2,1,0:T(8,128)} dynamic-update-slice(f32[2,768,1024]{2,1,0:T(8,128)} %get-tuple-element.214, f32[2,256,256]{2,1,0:T(8,128)S(1)} %bitcast_add_fusion.2, s32[]{:T(128)} %constant.56.clone.1..sunk, s32[]{:T(128)S(6)} %select_n.104, s32[]{:T(128)S(6)} %select_n.105) | dynamic-update-slice | bytes 1048580 | tf_op jit(solution)/shard_map/while/body/eval_jaxpr/dynamic_update_slice | solution.py:89
  297.7 6.1 %dynamic_update_slice.8 = f32[2,768,1024]{2,1,0:T(8,128)} dynamic-update-slice(f32[2,768,1024]{2,1,0:T(8,128)} %get-tuple-element.214, f32[2,256,256]{2,1,0:T(8,128)S(1)} %bitcast_add_fusion.2, s32[]{:T(128)} %constant.56.clone.1..sunk, s32[]{:T(128)S(6)} %select_n.104, s32[]{:T(128)S(6)} %select_n.105) | dynamic-update-slice | bytes 1048580 | tf_op jit(solution)/shard_map/while/body/eval_jaxpr/dynamic_update_slice | solution.py:89
  310.0 6.8 %dynamic_update_slice.8 = f32[2,768,1024]{2,1,0:T(8,128)} dynamic-update-slice(f32[2,768,1024]{2,1,0:T(8,128)} %get-tuple-element.214, f32[2,256,256]{2,1,0:T(8,128)S(1)} %bitcast_add_fusion.2, s32[]{:T(128)} %constant.56.clone.1..sunk, s32[]{:T(128)S(6)} %select_n.104, s32[]{:T(128)S(6)} %select_n.105) | dynamic-update-slice | bytes 1048580 | tf_op jit(solution)/shard_map/while/body/eval_jaxpr/dynamic_update_slice | solution.py:89
  323.0 6.5 %dynamic_update_slice.8 = f32[2,768,1024]{2,1,0:T(8,128)} dynamic-update-slice(f32[2,768,1024]{2,1,0:T(8,128)} %get-tuple-element.214, f32[2,256,256]{2,1,0:T(8,128)S(1)} %bitcast_add_fusion.2, s32[]{:T(128)} %constant.56.clone.1..sunk, s32[]{:T(128)S(6)} %select_n.104, s32[]{:T(128)S(6)} %select_n.105) | dynamic-update-slice | bytes 1048580 | tf_op jit(solution)/shard_map/while/body/eval_jaxpr/dynamic_update_slice | solution.py:89
  335.7 6.8 %dynamic_update_slice.8 = f32[2,768,1024]{2,1,0:T(8,128)} dynamic-update-slice(f32[2,768,1024]{2,1,0:T(8,128)} %get-tuple-element.214, f32[2,256,256]{2,1,0:T(8,128)S(1)} %bitcast_add_fusion.2, s32[]{:T(128)} %constant.56.clone.1..sunk, s32[]{:T(128)S(6)} %select_n.104, s32[]{:T(128)S(6)} %select_n.105) | dynamic-update-slice | bytes 1048580 | tf_op jit(solution)/shard_map/while/body/eval_jaxpr/dynamic_update_slice | solution.py:89
  348.6 6.7 %dynamic_update_slice.8 = f32[2,768,1024]{2,1,0:T(8,128)} dynamic-update-slice(f32[2,768,1024]{2,1,0:T(8,128)} %get-tuple-element.214, f32[2,256,256]{2,1,0:T(8,128)S(1)} %bitcast_add_fusion.2, s32[]{:T(128)} %constant.56.clone.1..sunk, s32[]{:T(128)S(6)} %select_n.104, s32[]{:T(128)S(6)} %select_n.105) | dynamic-update-slice | bytes 1048580 | tf_op jit(solution)/shard_map/while/body/eval_jaxpr/dynamic_update_slice | solution.py:89
  361.5 6.8 %dynamic_update_slice.8 = f32[2,768,1024]{2,1,0:T(8,128)} dynamic-update-slice(f32[2,768,1024]{2,1,0:T(8,128)} %get-tuple-element.214, f32[2,256,256]{2,1,0:T(8,128)S(1)} %bitcast_add_fusion.2, s32[]{:T(128)} %constant.56.clone.1..sunk, s32[]{:T(128)S(6)} %select_n.104, s32[]{:T(128)S(6)} %select_n.105) | dynamic-update-slice | bytes 1048580 | tf_op jit(solution)/shard_map/while/body/eval_jaxpr/dynamic_update_slice | solution.py:89
  368.3 1.7 slice.41
  370.0 1.9 collective-permute-start.1
  372.0 23.0 %collective-permute-done.1 = f32[2,256,1024]{2,1,0:T(8,128)S(1)} collective-permute-done((f32[2,256,1024]{2,1,0:T(8,128)S(1)}, f32[2,256,1024]{2,1,0:T(8,128)S(1)}, u32[]{:S(2)}, u32[]{:S(2)}) %collective-permute-start.1) | collective-permute-done | bytes 2097184 | tf_op jit(solution)/shard_map/ppermute | solution.py:11
  394.9 5.1 pad_add_fusion
  400.1 7.7 %reduce_sum.29 = f32[2,256,256]{2,1,0:T(8,128)} reduce(f32[32,2,256,256]{3,2,1,0:T(8,128)} %bitcast.136, f32[]{:T(128)} %constant.57.clone.1), dimensions={0}, to_apply=%region_5.6 | reduce | flops 4063232 | bytes 17301508 | tf_op jit(solution)/shard_map/reduce_sum | solution.py:81
  407.8 119.6 %reduce-scatter.2.cloned.1.call-done = f32[2,512,128]{2,1,0:T(8,128)} async-done(((f32[2,512,1024]{2,1,0:T(8,128)}), f32[2,512,128]{2,1,0:T(8,128)}) %reduce-scatter.2.cloned.1.call-update) | async-done | bytes 524304 | tf_op jit(solution)/shard_map/reduce_scatter | solution.py:100
  (86 shorter events, 46.2 us)
Async XLA Ops:
  8.0 7.6 %copy-start.2 = (s32[16,2]{0,1:T(2,128)S(1)}, s32[16,2]{0,1:T(2,128)}, u32[]{:S(2)}) copy-start(s32[16,2]{0,1:T(2,128)} %param.10) | copy-start | bytes 388
  8.0 7.7 %copy-start.1 = (f32[1,2,256,256]{3,2,1,0:T(8,128)S(1)}, f32[1,2,256,256]{3,2,1,0:T(8,128)}, u32[]{:S(2)}) copy-start(f32[1,2,256,256]{3,2,1,0:T(8,128)} %param.8) | copy-start | bytes 1572868
  8.0 392.0 %all-gather.3.cloned.1.call-start = ((), (), s32[]{:S(2)}) async-start(), calls=%async_computation.2 | async-start | bytes 17301504 | tf_op jit(solution)/shard_map/all_gather | solution.py:80
  9.8 28.4 %collective-permute-start = (f32[2,256,1024]{2,1,0:T(8,128)S(1)}, f32[2,256,1024]{2,1,0:T(8,128)}, u32[]{:S(2)}, u32[]{:S(2)}) collective-permute-start(f32[2,256,1024]{2,1,0:T(8,128)S(1)} %slice.34), channel_id=1, source_target_pairs={{1,0},{2,1},{3,2},{4,3},{5,4},{6,5},{7,6},{8,7},{9,8},{10,9},{11,1... | collective-permute-start | bytes 6291464 | tf_op jit(solution)/shard_map/ppermute | solution.py:11
  126.3 1.9 copy-start
  139.5 3.4 slice-start
  141.2 2.3 slice-start.1
  151.8 375.6 %reduce-scatter.2.cloned.1.call-start = ((), (), s32[]{:S(2)}) async-start(), calls=%async_computation.1 | async-start | bytes 4718592 | tf_op jit(solution)/shard_map/reduce_scatter | solution.py:100
  370.0 24.9 %collective-permute-start.1 = (f32[2,256,1024]{2,1,0:T(8,128)S(1)}, f32[2,256,1024]{2,1,0:T(8,128)S(1)}, u32[]{:S(2)}, u32[]{:S(2)}) collective-permute-start(f32[2,256,1024]{2,1,0:T(8,128)S(1)} %slice.41), channel_id=1, source_target_pairs={{0,1},{1,2},{2,3},{3,4},{4,5},{5,6},{6,7},{7,8},{8,9},{9,10},{10,1... | collective-permute-start | bytes 6291464 | tf_op jit(solution)/shard_map/ppermute | solution.py:11
Sparse Core Ops, SparseCore 0:
  151.9 104.3 all-gather.2
Sparse Core Ops, SparseCore 1:
  400.1 127.2 reduce-scatter.1
